TPU v7x, 256 devices: a whole 4x4x8 slice. The times are simulated.
256 devices in a mesh: tok: 64 (over y, z, core), head: 4 (over x).
Axes of the slice: x: 4, y: 4, z: 8, core: 2. Of those that a mesh axis runs over, the one named last changes fastest.
Arguments:
- hidden: bfloat16 [2048, 2048], P('tok', 'head'), may hold values from -24 to 24
- attn_gain: float32 [2048], replicated, may hold values from 0.1 to 1.9
- w_query: bfloat16 [2048, 3072], P(None, 'head'), may hold values from -0.125 to 0.125
- w_latent: bfloat16 [2048, 576], P('head'), may hold values from -0.125 to 0.125
- w_key_up: bfloat16 [16, 128, 512], P('head'), may hold values from -0.5 to 0.5
- w_value_up: bfloat16 [16, 512, 128], P('head'), may hold values from -1 to 1
- w_out: bfloat16 [2048, 2048], P('head'), may hold values from -0.125 to 0.125
- latent_cache: bfloat16 [638976, 576], P(('tok', 'head')), may hold values from -6 to 6
- cache_lengths: int32 [2048], P('tok'), may hold values from 144 to 2048, as said below
- request_slot: int32 [2048], P('tok'), may hold values from 0 to 2047, as said below
- ffn_gain: float32 [2048], P('head'), may hold values from 0.1 to 1.9
- w_router: bfloat16 [2048, 64], P('head'), may hold values from -0.25 to 0.25
- routes: int32 [2048, 6], P('tok'), may hold values from 0 to 63, all different within a row; in each aligned block of 32 rows (0 to 31, 32 to 63, ...) at most 6 rows name the same one
- expert_gate: bfloat16 [64, 2048, 1408], P('tok', None, 'head'), may hold values from -0.125 to 0.125
- expert_up: bfloat16 [64, 2048, 1408], P('tok', None, 'head'), may hold values from -0.125 to 0.125
- expert_down: bfloat16 [64, 1408, 2048], P('tok', 'head'), may hold values from -0.15625 to 0.15625
Outputs:
- new_entry: bfloat16 [2048, 576], P('tok')
- attended: bfloat16 [2048, 2048], P('tok', 'head')
- expert_mix: bfloat16 [2048, 2048], P('tok', 'head')
Inputs may be any that keep to these rules, and one draw needn't show every extreme that they name: `request_slot`: a permutation of the 2048 slots; slot s lies on owner s // 32, so every owner holds 32 slots; the requests of one device name at most 1 slots of one owner, and every device reaches that bound. `cache_lengths`: the caches of an owner's slots lie end to end in slot order at the start of that owner's 9984 rows of latent_cache; they fill at most 9984 rows, and some owner fills all of them. `routes`: each row names 6 different experts; in the rows of one device no expert is named more than 6 times.
All inputs are finite; a program needn't handle non-finite values.
Results may differ from a plain program's by a relative error of at most 0.028.
Values may be sent and summed in bfloat16 or wider, within the bound.
No kernel may reach another device: no remote copies, remote signals or barrier semaphores. Data moves between devices by JAX's collectives and lax.ppermute only.
A program may use at most 128 MiB of HBM per device.

v0:
```python
import jax
import jax.numpy as jnp
from jax import lax
from jax.sharding import PartitionSpec as P

D = 2048
NOPE = 128
ROPE = 64
LATENT = 512
NORM_EPS = 1e-06


def rotate_pairs(values, places):
    halfway = values.shape[-1] // 2
    freqs = 10000.0 ** (-jnp.arange(halfway, dtype=jnp.float32) / halfway)
    angles = places.astype(jnp.float32).reshape(places.shape + (1,) * (values.ndim - 1)) * freqs
    cosine = jnp.cos(angles)
    sine = jnp.sin(angles)
    first_half = values[..., :halfway]
    second_half = values[..., halfway:]
    return jnp.concatenate(
        [first_half * cosine - second_half * sine, first_half * sine + second_half * cosine],
        axis=-1,
    )


def owner_attend(all_heads, owner_lengths, latent_cache, head_index, factor):
    slot_rows = all_heads.shape[0]
    total_heads = all_heads.shape[1]
    probe_width = all_heads.shape[2]
    key_rows = latent_cache.shape[0]
    starts = jnp.cumsum(owner_lengths) - owner_lengths
    places = head_index * key_rows + jnp.arange(key_rows, dtype=jnp.int32)
    inside = (places[None, :] >= starts[:, None]) & (
        places[None, :] < (starts + owner_lengths)[:, None]
    )
    scores = factor * jnp.einsum(
        "qc,pc->qp",
        all_heads.reshape(slot_rows * total_heads, probe_width),
        latent_cache,
        preferred_element_type=jnp.float32,
    )
    scores = scores.reshape(slot_rows, total_heads, key_rows)
    weights = jnp.where(inside[:, None, :], jnp.exp(scores), 0.0).astype(jnp.bfloat16)
    numerator = jnp.einsum(
        "khp,pl->khl", weights, latent_cache[:, :LATENT], preferred_element_type=jnp.float32
    )
    denominator = jnp.sum(weights.astype(jnp.float32), axis=2)
    return (numerator, denominator)


def body(
    hidden,
    attn_gain,
    w_query,
    w_latent,
    w_key_up,
    w_value_up,
    w_out,
    latent_cache,
    cache_lengths,
    request_slot,
    ffn_gain,
    w_router,
    routes,
    expert_gate,
    expert_up,
    expert_down,
):
    local_rows = hidden.shape[0]
    quarter_width = hidden.shape[1]
    local_heads = w_key_up.shape[0]
    peer_count = lax.axis_size("tok")
    head_index = lax.axis_index("head")
    tok_index = lax.axis_index("tok")
    row_ids = jnp.arange(local_rows, dtype=jnp.int32)
    gathered = lax.all_gather(hidden, "head", axis=1, tiled=True)
    widened = gathered.astype(jnp.float32)
    inv_attn = lax.rsqrt(jnp.mean(widened * widened, axis=1, keepdims=True) + NORM_EPS)
    normed_attn = (widened * inv_attn * attn_gain).astype(jnp.bfloat16)
    normed_part = lax.dynamic_slice_in_dim(
        normed_attn, head_index * quarter_width, quarter_width, 1
    )
    compressed = lax.psum(
        jnp.dot(normed_part, w_latent, preferred_element_type=jnp.float32), "head"
    )
    latent_new = compressed[:, :LATENT]
    latent_new = latent_new * lax.rsqrt(
        jnp.mean(latent_new * latent_new, axis=1, keepdims=True) + NORM_EPS
    )
    new_entry = jnp.concatenate(
        [latent_new, rotate_pairs(compressed[:, LATENT:], cache_lengths)], axis=1
    ).astype(jnp.bfloat16)
    queries = jnp.dot(normed_attn, w_query, preferred_element_type=jnp.float32).astype(jnp.bfloat16)
    queries = queries.reshape(local_rows, local_heads, NOPE + ROPE)
    absorbed = jnp.einsum(
        "bhn,hnl->bhl", queries[:, :, :NOPE], w_key_up, preferred_element_type=jnp.float32
    ).astype(jnp.bfloat16)
    turned = rotate_pairs(queries[:, :, NOPE:].astype(jnp.float32), cache_lengths).astype(
        jnp.bfloat16
    )
    probes = jnp.concatenate([absorbed, turned], axis=2)
    factor = (NOPE + ROPE) ** (-0.5)
    self_score = factor * jnp.einsum(
        "bhc,bc->bh", probes, new_entry, preferred_element_type=jnp.float32
    )
    self_weight = jnp.exp(self_score).astype(jnp.bfloat16).astype(jnp.float32)
    per_owner = max(1, local_rows // peer_count)
    buffer_rows = peer_count * per_owner
    buffer_ids = jnp.arange(buffer_rows, dtype=jnp.int32)
    dest_owner = request_slot // local_rows
    earlier_same = (dest_owner[None, :] == dest_owner[:, None]) & (
        row_ids[None, :] < row_ids[:, None]
    )
    send_place = dest_owner * per_owner + jnp.sum(earlier_same.astype(jnp.int32), axis=1)
    all_probes, all_slots, all_lengths = (
        lax.all_gather(probes, "tok", axis=0, tiled=True),
        lax.all_gather(request_slot, "tok", axis=0, tiled=True),
        lax.all_gather(cache_lengths, "tok", axis=0, tiled=True),
    )
    total_rows = all_slots.shape[0]
    slot_hit = all_slots[None, :] == (tok_index * local_rows + row_ids)[:, None]
    request_at = jnp.sum(
        jnp.where(slot_hit, jnp.arange(total_rows, dtype=jnp.int32)[None, :], 0), axis=1
    )
    owner_probes = all_probes[request_at]
    owner_lengths = all_lengths[request_at]
    owned_here = (
        (all_slots // local_rows == tok_index).astype(jnp.int32).reshape(peer_count, local_rows)
    )
    prior_count = (jnp.cumsum(owned_here, axis=1) - owned_here).reshape(total_rows)
    back_index = request_at // local_rows * per_owner + prior_count[request_at]
    all_heads = lax.all_gather(owner_probes, "head", axis=1, tiled=True)
    numerator, denominator = owner_attend(
        all_heads, owner_lengths, latent_cache, head_index, factor
    )
    group_num, group_den = (
        lax.psum_scatter(numerator, "head", scatter_dimension=1, tiled=True),
        lax.psum_scatter(denominator, "head", scatter_dimension=1, tiled=True),
    )
    at_place = buffer_ids[:, None] == back_index[None, :]
    slot_of_place = jnp.sum(jnp.where(at_place, row_ids[None, :], 0), axis=1) + local_rows * (
        1 - jnp.max(at_place.astype(jnp.int32), axis=1)
    )
    padded_num = jnp.concatenate(
        [group_num, jnp.zeros((1, local_heads, LATENT), jnp.float32)], axis=0
    )
    padded_den = jnp.concatenate([group_den, jnp.zeros((1, local_heads), jnp.float32)], axis=0)
    got_num, got_den = (
        lax.all_to_all(
            padded_num[slot_of_place].reshape(peer_count, per_owner, local_heads, LATENT),
            "tok",
            split_axis=0,
            concat_axis=0,
            tiled=True,
        ),
        lax.all_to_all(
            padded_den[slot_of_place].reshape(peer_count, per_owner, local_heads),
            "tok",
            split_axis=0,
            concat_axis=0,
            tiled=True,
        ),
    )
    back_num = got_num.reshape(buffer_rows, local_heads, LATENT)
    back_den = got_den.reshape(buffer_rows, local_heads)
    total_num = back_num[send_place] + self_weight[:, :, None] * new_entry[:, None, :LATENT].astype(
        jnp.float32
    )
    total_den = back_den[send_place] + self_weight
    mixed_latent = (total_num / total_den[:, :, None]).astype(jnp.bfloat16)
    head_out = jnp.einsum(
        "bhl,hld->bhd", mixed_latent, w_value_up, preferred_element_type=jnp.float32
    ).astype(jnp.bfloat16)
    head_out = head_out.reshape(local_rows, local_heads * NOPE)
    attn_piece = lax.psum_scatter(
        jnp.dot(head_out, w_out, preferred_element_type=jnp.float32),
        "head",
        scatter_dimension=1,
        tiled=True,
    )
    attended = (hidden.astype(jnp.float32) + attn_piece).astype(jnp.bfloat16)
    attended_wide = attended.astype(jnp.float32)
    gained = (attended_wide * ffn_gain).astype(jnp.bfloat16)
    squares, logit_part = lax.psum(
        (
            jnp.sum(attended_wide * attended_wide, axis=1),
            jnp.dot(gained, w_router, preferred_element_type=jnp.float32),
        ),
        "head",
    )
    inv_ffn = lax.rsqrt(squares / D + NORM_EPS)
    logits = logit_part * inv_ffn[:, None]
    normed_ffn = (attended_wide * ffn_gain * inv_ffn[:, None]).astype(jnp.bfloat16)
    expert_count = w_router.shape[1]
    route_count = routes.shape[1]
    expert_ids = jnp.arange(expert_count, dtype=jnp.int32)
    named = routes[:, :, None] == expert_ids[None, None, :]
    picked = jnp.sum(jnp.where(named, logits[:, None, :], 0.0), axis=2)
    lifted = jnp.exp(picked)
    route_weight = lifted / jnp.sum(lifted, axis=1, keepdims=True)
    struck = jnp.max(named.astype(jnp.int32), axis=1)
    earlier_hits = jnp.cumsum(struck, axis=0) - struck
    capacity = min(local_rows, max(2, 2 * local_rows * route_count // expert_count))
    route_place = routes * capacity + jnp.take_along_axis(earlier_hits, routes, axis=1)
    slot_total = expert_count * capacity
    slot_ids = jnp.arange(slot_total, dtype=jnp.int32)
    filled = route_place[None, :, :] == slot_ids[:, None, None]
    source_token = jnp.sum(
        jnp.where(filled, row_ids[None, :, None], 0), axis=(1, 2)
    ) + local_rows * (1 - jnp.max(filled.astype(jnp.int32), axis=(1, 2)))
    full_rows = lax.all_gather(normed_ffn, "head", axis=1, tiled=True)
    padded_rows = jnp.concatenate(
        [full_rows, jnp.zeros((1, full_rows.shape[1]), jnp.bfloat16)], axis=0
    )
    arrived = lax.all_to_all(
        padded_rows[source_token].reshape(expert_count, capacity, full_rows.shape[1]),
        "tok",
        split_axis=0,
        concat_axis=0,
        tiled=True,
    )
    expert_in = arrived.reshape(peer_count * capacity, full_rows.shape[1])
    gate_value = jnp.dot(expert_in, expert_gate[0], preferred_element_type=jnp.float32)
    up_value = jnp.dot(expert_in, expert_up[0], preferred_element_type=jnp.float32)
    activity = (jax.nn.silu(gate_value) * up_value).astype(jnp.bfloat16)
    expert_share = lax.psum_scatter(
        jnp.dot(activity, expert_down[0], preferred_element_type=jnp.float32).astype(jnp.bfloat16),
        "head",
        scatter_dimension=1,
        tiled=True,
    )
    returned = lax.all_to_all(
        expert_share.reshape(peer_count, capacity, quarter_width),
        "tok",
        split_axis=0,
        concat_axis=0,
        tiled=True,
    )
    chosen_rows = returned.reshape(slot_total, quarter_width)[route_place]
    expert_mix = jnp.sum(route_weight[:, :, None] * chosen_rows.astype(jnp.float32), axis=1).astype(
        jnp.bfloat16
    )
    return (new_entry, attended, expert_mix)


def solution(mesh):
    in_specs = (
        P("tok", "head"),
        P(),
        P(None, "head"),
        P("head", None),
        P("head", None, None),
        P("head", None, None),
        P("head", None),
        P(("tok", "head"), None),
        P("tok"),
        P("tok"),
        P("head"),
        P("head", None),
        P("tok", None),
        P("tok", None, "head"),
        P("tok", None, "head"),
        P("tok", "head", None),
    )
    out_specs = (P("tok", None), P("tok", "head"), P("tok", "head"))
    return jax.shard_map(body, mesh=mesh, in_specs=in_specs, out_specs=out_specs, check_vma=False)
```

profile of v0, /device:TPU:1, one launch (start us, length us, event | category | flops | bytes accessed | tf_op | source)
XLA Modules:
  0.0 640.7 jit_solution(2848119772154112607)
XLA Ops:
  7.2 10.6 %all_gather.18 = bf16[32,2048]{1,0:T(8,128)(2,1)S(1)} all-gather(bf16[32,512]{1,0:T(8,128)(2,1)} %param.16), channel_id=1, replica_groups=mesh['tok'=64,'head'=4] {'head'}, dimensions={1}, use_global_device_ids=true | all-gather | bytes 163840 | tf_op jit(solution)/shard_map/all_gather | solution.py:77
  18.0 0.8 fusion.28
  18.8 2.0 fusion.45
  21.8 1.2 fusion.16
  23.0 46.7 %all-reduce.10.cloned.1.call-done = f32[32,576]{1,0:T(8,128)} async-done(((f32[32,576]{1,0:T(8,128)}), f32[32,576]{1,0:T(8,128)}) %all-reduce.10.cloned.1.call-update) | async-done | bytes 73744 | tf_op jit(solution)/shard_map/psum | solution.py:84
  69.7 1.5 multiply_cosine_fusion
  74.0 246.6 %all-reduce.6 = (s32[2048]{0:T(1024)S(1)}, s32[2048]{0:T(1024)S(1)}) all-reduce(s32[2048]{0:T(1024)S(1)} %dynamic-update-slice.1, s32[2048]{0:T(1024)S(1)} %dynamic-update-slice), channel_id=1, replica_groups=mesh['tok'=64,'head'=4] {'tok'}, use_global_device_ids=true, to_apply=%add.4 | all-reduce | flops 4096 | bytes 32768
  322.4 2.4 copy.92
  324.8 14.7 %copy.84 = bf16[2048,4,576]{2,1,0:T(4,128)(2,1)} copy(bf16[2048,4,576]{2,0,1:T(8,128)(2,1)} %all-gather.3.cloned.1.call-done) | data formatting | bytes 18874368 | tf_op jit(solution)/shard_map/all_gather | solution.py:117
  339.5 4.7 gather_fusion.1
  344.3 10.5 %all-gather = bf16[32,16,576]{2,0,1:T(8,128)(2,1)S(1)} all-gather(bf16[32,4,576]{2,0,1:T(8,128)(2,1)S(1)} %copy.85), channel_id=2, replica_groups=mesh['tok'=64,'head'=4] {'head'}, dimensions={1}, use_global_device_ids=true | all-gather | bytes 737280 | tf_op jit(solution)/shard_map/all_gather | solution.py:133
  355.0 6.3 convert_reduce_fusion
  361.3 4.4 copy.87
  365.7 4.1 fusion
  369.8 1.6 copy.89
  374.4 13.0 %all-reduce.5 = f32[32,16]{1,0:T(8,128)S(1)} all-reduce(f32[32,16]{1,0:T(8,128)S(1)} %reduce_sum.110), channel_id=4, replica_groups=mesh['tok'=64,'head'=4] {'head'}, use_global_device_ids=true, to_apply=%region_11.12.clone | all-reduce | flops 512 | bytes 4096
  387.5 1.2 gather_fusion.5
  388.7 16.3 %all-to-all-start.1 = ((f32[64,1,4]{2,1,0:T(1,128)}), f32[64,1,4]{2,1,0:T(1,128)S(1)}, u32[]{:S(2)}, u32[]{:S(2)}) async-start(f32[64,1,4]{2,1,0:T(1,128)} %bitcast.18), calls=%async_computation.2 | async-start | bytes 65536 | tf_op jit(solution)/shard_map/all_to_all | solution.py:157
  405.8 1.6 gather_fusion.9
  408.1 1.1 copy.90
  409.3 1.8 gather_fusion.3
  411.1 3.3 all-to-all-done.1
  414.4 7.3 %all-to-all-start = ((f32[64,1,4,512]{3,2,1,0:T(4,128)}), f32[64,1,4,512]{3,2,1,0:T(4,128)}, u32[]{:S(2)}, u32[]{:S(2)}) async-start(f32[64,1,4,512]{3,2,1,0:T(4,128)} %bitcast.72), calls=%async_computation.1 | async-start | bytes 1048576 | tf_op jit(solution)/shard_map/all_to_all | solution.py:150
  423.2 0.8 fusion.73
  424.0 1.2 fusion.30
  426.5 12.4 %all-to-all-done = f32[64,1,4,512]{3,2,1,0:T(4,128)} async-done(((f32[64,1,4,512]{3,2,1,0:T(4,128)}), f32[64,1,4,512]{3,2,1,0:T(4,128)}, u32[]{:S(2)}, u32[]{:S(2)}) %all-to-all-start) | async-done | bytes 524320 | tf_op jit(solution)/shard_map/all_to_all | solution.py:150
  438.9 1.9 gather_fusion.4
  440.8 1.0 fusion.29
  441.9 1.2 fusion.17
  443.2 2.8 fusion.40
  447.0 14.9 %reduce-scatter.7.cloned.1.call-done = f32[32,512]{1,0:T(8,128)} async-done(((f32[32,2048]{1,0:T(8,128)}), f32[32,512]{1,0:T(8,128)}) %reduce-scatter.7.cloned.1.call-update) | async-done | bytes 65552 | tf_op jit(solution)/shard_map/reduce_scatter | solution.py:176
  461.9 1.0 fusion.37
  463.1 11.8 %all-reduce.7 = (f32[32]{0:T(128)S(1)}, f32[32,64]{1,0:T(8,128)S(1)}) all-reduce(f32[32]{0:T(128)S(1)} %get-tuple-element.13, f32[32,64]{1,0:T(8,128)S(1)} %fusion.38), channel_id=1, replica_groups=mesh['tok'=64,'head'=4] {'head'}, use_global_device_ids=true, to_apply=%region_15.16 | all-reduce | flops 2080 | bytes 16640 | tf_op jit(solution)/shard_map/psum | solution.py:185
  474.9 9.3 %all_gather.23 = bf16[32,2048]{1,0:T(8,128)(2,1)S(1)} all-gather(bf16[32,512]{1,0:T(8,128)(2,1)S(1)} %fusion.36), channel_id=1, replica_groups=mesh['tok'=64,'head'=4] {'head'}, dimensions={1}, use_global_device_ids=true | all-gather | bytes 163840 | tf_op jit(solution)/shard_map/all_gather | solution.py:212
  484.3 3.1 gather_fusion.7
  487.4 3.7 reshape.358
  491.1 70.4 %all_to_all.20 = bf16[64,6,2048]{2,1,0:T(8,128)(2,1)} all-to-all(bf16[64,6,2048]{2,1,0:T(8,128)(2,1)} %reshape.358), channel_id=1, replica_groups=mesh['tok'=64,'head'=4] {'tok'}, dimensions={0} | all-to-all | bytes 3145728 | tf_op jit(solution)/shard_map/all_to_all | solution.py:216
  561.5 3.7 reshape.359
  565.3 3.6 fusion.8
  568.8 5.5 convolution_convert_fusion
  574.5 22.3 %reduce-scatter.9.cloned.1.call-done = bf16[384,512]{1,0:T(8,128)(2,1)} async-done(((bf16[384,2048]{1,0:T(8,128)(2,1)}), bf16[384,512]{1,0:T(8,128)(2,1)}) %reduce-scatter.9.cloned.1.call-update) | async-done | bytes 393232 | tf_op jit(solution)/shard_map/reduce_scatter | solution.py:227
  596.8 1.9 reshape.360
  598.7 11.7 %all-to-all-start.3 = ((bf16[64,6,512]{2,1,0:T(8,128)(2,1)}), bf16[64,6,512]{2,1,0:T(8,128)(2,1)}, u32[]{:S(2)}, u32[]{:S(2)}) async-start(bf16[64,6,512]{2,1,0:T(8,128)(2,1)} %reshape.360), calls=%async_computation.6 | async-start | bytes 1048576 | tf_op jit(solution)/shard_map/all_to_all | solution.py:233
  612.1 15.5 %all-to-all-done.3 = bf16[64,6,512]{2,1,0:T(8,128)(2,1)} async-done(((bf16[64,6,512]{2,1,0:T(8,128)(2,1)}), bf16[64,6,512]{2,1,0:T(8,128)(2,1)}, u32[]{:S(2)}, u32[]{:S(2)}) %all-to-all-start.3) | async-done | bytes 393248 | tf_op jit(solution)/shard_map/all_to_all | solution.py:233
  627.6 1.2 reshape.361
  628.8 1.7 gather_fusion.8
  630.5 1.8 reshape.445
  632.2 1.9 multiply_reduce_fusion
  (127 shorter events, 14.8 us)
Async XLA Ops:
  7.2 13.8 %copy-start = (bf16[2048,768]{1,0:T(8,128)(2,1)S(1)}, bf16[2048,768]{1,0:T(8,128)(2,1)}, u32[]{:S(2)}) copy-start(bf16[2048,768]{1,0:T(8,128)(2,1)} %param.18) | copy-start | bytes 9437188
  7.2 62.6 %all-reduce.10.cloned.1.call-start = ((), (), s32[]{:S(2)}) async-start(), calls=%async_computation.7 | async-start | bytes 163840 | tf_op jit(solution)/shard_map/psum | solution.py:84
  18.8 2.9 copy-start.14
  20.8 51.4 %copy-start.17 = (u32[256]{0:T(256)S(1)}, u32[256]{0:T(256)}, u32[]{:S(2)}) copy-start(u32[256]{0:T(256)} %constant.148) | copy-start | bytes 3076
  20.9 52.9 %copy-start.15 = (s32[32]{0:T(128)S(1)}, s32[32]{0:T(128)}, u32[]{:S(2)}) copy-start(s32[32]{0:T(128)} %param.25) | copy-start | bytes 388
  20.9 303.9 %all-gather.3.cloned.1.call-start = ((), (), s32[]{:S(2)}) async-start(), calls=%async_computation.8 | async-start | bytes 10649600 | tf_op jit(solution)/shard_map/all_gather | solution.py:117
  72.1 336.0 %reduce-scatter.5.cloned.1.call-start = ((), (), s32[]{:S(2)}) async-start(), calls=%async_computation.9 | async-start | bytes 1310720 | tf_op jit(solution)/shard_map/reduce_scatter | solution.py:138
  344.2 10.7 %copy-start.1 = (pred[512,2496]{0,1:T(32,128)(4,1)S(1)}, pred[512,2496]{0,1:T(32,128)(4,1)}, u32[]{:S(2)}) copy-start(pred[512,2496]{0,1:T(32,128)(4,1)} %copy.92) | copy-start | bytes 3833860
  369.8 1.7 copy-start.9
  369.8 2.8 copy-start.16
  374.0 31.8 %copy-start.13 = (s32[1024]{0:T(1024)}, s32[1024]{0:T(1024)S(1)}, u32[]{:S(2)}) copy-start(s32[1024]{0:T(1024)S(1)} %pad_clamp_fusion.3) | copy-start | bytes 12292
  388.7 25.7 %all-to-all-start.1 = ((f32[64,1,4]{2,1,0:T(1,128)}), f32[64,1,4]{2,1,0:T(1,128)S(1)}, u32[]{:S(2)}, u32[]{:S(2)}) async-start(f32[64,1,4]{2,1,0:T(1,128)} %bitcast.18), calls=%async_computation.2 | async-start | bytes 65536 | tf_op jit(solution)/shard_map/all_to_all | solution.py:157
  407.4 14.4 %copy-start.2 = (f32[32,576]{1,0:T(8,128)S(1)}, f32[32,576]{1,0:T(8,128)}, u32[]{:S(2)}) copy-start(f32[32,576]{1,0:T(8,128)} %all-reduce.10.cloned.1.call-done) | copy-start | bytes 221188
  414.4 24.5 %all-to-all-start = ((f32[64,1,4,512]{3,2,1,0:T(4,128)}), f32[64,1,4,512]{3,2,1,0:T(4,128)}, u32[]{:S(2)}, u32[]{:S(2)}) async-start(f32[64,1,4,512]{3,2,1,0:T(4,128)} %bitcast.72), calls=%async_computation.1 | async-start | bytes 1048576 | tf_op jit(solution)/shard_map/all_to_all | solution.py:150
  421.7 40.2 %reduce-scatter.7.cloned.1.call-start = ((), (), s32[]{:S(2)}) async-start(), calls=%async_computation.10 | async-start | bytes 327680 | tf_op jit(solution)/shard_map/reduce_scatter | solution.py:176
  422.6 0.6 copy-start.4
  440.8 21.1 %copy-start.6 = (bf16[32,512]{1,0:T(8,128)(2,1)S(1)}, bf16[32,512]{1,0:T(8,128)(2,1)}, u32[]{:S(2)}) copy-start(bf16[32,512]{1,0:T(8,128)(2,1)} %param.16) | copy-start | bytes 98308
  440.8 22.1 %copy-start.8 = (bf16[512,64]{0,1:T(8,128)(2,1)S(1)}, bf16[512,64]{0,1:T(8,128)(2,1)}, u32[]{:S(2)}) copy-start(bf16[512,64]{0,1:T(8,128)(2,1)} %param.27) | copy-start | bytes 196612
  440.8 22.1 %copy-start.11 = (f32[512]{0:T(512)S(1)}, f32[512]{0:T(512)}, u32[]{:S(2)}) copy-start(f32[512]{0:T(512)} %param.26) | copy-start | bytes 6148
  441.9 33.0 %copy-start.12 = (f32[512]{0:T(512)S(1)}, f32[512]{0:T(512)}, u32[]{:S(2)}) copy-start(f32[512]{0:T(512)} %param.26) | copy-start | bytes 6148
  445.9 150.9 %reduce-scatter.9.cloned.1.call-start = ((), (), s32[]{:S(2)}) async-start(), calls=%async_computation.11 | async-start | bytes 1966080 | tf_op jit(solution)/shard_map/reduce_scatter | solution.py:227
  462.9 12.0 %copy-start.3 = (bf16[32,512]{1,0:T(8,128)(2,1)}, bf16[32,512]{1,0:T(8,128)(2,1)S(1)}, u32[]{:S(2)}) copy-start(bf16[32,512]{1,0:T(8,128)(2,1)S(1)} %get-tuple-element.14) | copy-start | bytes 98308
  574.3 36.1 %copy-start.5 = (bf16[32,512]{1,0:T(8,128)(2,1)S(1)}, bf16[32,512]{1,0:T(8,128)(2,1)}, u32[]{:S(2)}) copy-start(bf16[32,512]{1,0:T(8,128)(2,1)} %copy-done.4) | copy-start | bytes 98308
  574.3 36.1 %copy-start.7 = (bf16[32,32]{1,0:T(8,128)(2,1)S(1)}, bf16[32,32]{1,0:T(8,128)(2,1)}, u32[]{:S(2)}) copy-start(bf16[32,32]{1,0:T(8,128)(2,1)} %get-tuple-element.26) | copy-start | bytes 6148
  574.3 36.9 %copy-start.10 = (s32[32,6]{0,1:T(8,128)S(1)}, s32[32,6]{0,1:T(8,128)}, u32[]{:S(2)}) copy-start(s32[32,6]{0,1:T(8,128)} %param.28) | copy-start | bytes 2308
  598.7 28.9 %all-to-all-start.3 = ((bf16[64,6,512]{2,1,0:T(8,128)(2,1)}), bf16[64,6,512]{2,1,0:T(8,128)(2,1)}, u32[]{:S(2)}, u32[]{:S(2)}) async-start(bf16[64,6,512]{2,1,0:T(8,128)(2,1)} %reshape.360), calls=%async_computation.6 | async-start | bytes 1048576 | tf_op jit(solution)/shard_map/all_to_all | solution.py:233
Sparse Core Ops, SparseCore 0:
  21.0 48.7 all-reduce.9
  72.5 89.3 all-gather.2
  371.5 25.9 reduce-scatter.4
  446.1 15.8 reduce-scatter.6
  574.5 22.2 reduce-scatter.8
where the time goes:
time: 642 us; the launch traced here: 641 us
  blocking collectives  372 us (58%)
  waiting for transfers between devices  115 us (18%)
  local copies, waits for them, and re-layouts  60 us (9%)
  starting transfers between devices  35.5 us (6%)
  matrix products  28.6 us (4%)
  between operations  15.6 us (2%)
  other arithmetic  13.3 us (2%)
    unnamed x2, blocking collectives  260 us
    all_to_all x1, blocking collectives, body(): lax.all_to_all(padded_rows[source_token].reshape(expert_count, capacity,...  70.4 us
    psum x1, waiting for transfers between devices, body(): lax.psum(jnp.dot(normed_part, w_latent, preferred_element_type=jnp.float3...  46.7 us
    reduce_scatter x1, waiting for transfers between devices, body(): lax.psum_scatter(jnp.dot(activity, expert_down[0], preferred_element_type...  22.3 us
    all_to_all x1, starting transfers between devices, body(): lax.all_to_all(padded_den[slot_of_place].reshape(peer_count, per_owner, l...  16.3 us
    all_to_all x1, waiting for transfers between devices, body(): lax.all_to_all(expert_share.reshape(peer_count, capacity, quarter_width),...  15.5 us
    reduce_scatter x1, waiting for transfers between devices, body(): lax.psum_scatter(jnp.dot(head_out, w_out, preferred_element_type=jnp.floa...  14.9 us
    all_gather x1, local copies, waits for them, and re-layouts, body(): lax.all_gather(probes, 'tok', axis=0, tiled=True)  14.7 us
  transfers between devices with their start and end apart: 8, of which 6 were waited for; matrix products, arithmetic and copies ran while one was open for 4% of the time, Pallas kernels for 0%

commit v1 on v0

--- a/solution.py
+++ b/solution.py
@@ -81,8 +81,9 @@
     normed_part = lax.dynamic_slice_in_dim(
         normed_attn, head_index * quarter_width, quarter_width, 1
     )
-    compressed = lax.psum(
-        jnp.dot(normed_part, w_latent, preferred_element_type=jnp.float32), "head"
+    compressed = jnp.sum(
+        lax.all_gather(jnp.dot(normed_part, w_latent, preferred_element_type=jnp.float32), "head"),
+        axis=0,
     )
     latent_new = compressed[:, :LATENT]
     latent_new = latent_new * lax.rsqrt(

time: 642 us -> 615 us (0.958)
  waiting for transfers between devices: 115 us -> 70.9 us
  blocking collectives: 372 us -> 387 us
    psum x1 -> x0, waiting for transfers between devices: 46.7 us -> none  [body(): lax.psum(jnp.dot(normed_part, w_latent, preferred_element_type=jnp.float3...]
    all_gather x0 -> x1, blocking collectives: none -> 9.51 us  [body(): lax.all_gather(jnp.dot(normed_part, w_latent, preferred_element_type=jnp....]
  transfers between devices with their start and end apart: 8 -> 7, of which waited for: 6 -> 5; matrix products, arithmetic and copies ran while one was open for 4% -> 4% of each run, Pallas kernels for 0% -> 0%
where the time goes in v1:
time: 615 us; the launch traced here: 613 us
  blocking collectives  387 us (63%)
  waiting for transfers between devices  70.9 us (12%)
  local copies, waits for them, and re-layouts  63.2 us (10%)
  starting transfers between devices  32.7 us (5%)
  matrix products  27.8 us (5%)
  other arithmetic  16.2 us (3%)
  between operations  15.7 us (3%)
    unnamed x2, blocking collectives  265 us
    all_to_all x1, blocking collectives, body(): lax.all_to_all(padded_rows[source_token].reshape(expert_count, capacity,...  70.4 us
    reduce_scatter x1, waiting for transfers between devices, body(): lax.psum_scatter(jnp.dot(activity, expert_down[0], preferred_element_type...  21.6 us
    all_to_all x1, waiting for transfers between devices, body(): lax.all_to_all(expert_share.reshape(peer_count, capacity, quarter_width),...  16.2 us
    all_to_all x1, starting transfers between devices, body(): lax.all_to_all(padded_den[slot_of_place].reshape(peer_count, per_owner, l...  15.3 us
    reduce_scatter x1, waiting for transfers between devices, body(): lax.psum_scatter(jnp.dot(head_out, w_out, preferred_element_type=jnp.floa...  15 us
    all_gather x1, local copies, waits for them, and re-layouts, body(): lax.all_gather(probes, 'tok', axis=0, tiled=True)  14.8 us
  transfers between devices with their start and end apart: 7, of which 5 were waited for; matrix products, arithmetic and copies ran while one was open for 4% of the time, Pallas kernels for 0%

profile of v1, /device:TPU:1, one launch (start us, length us, event | category | flops | bytes accessed | tf_op | source)
XLA Modules:
  0.0 613.4 jit_solution(11631702008648657482)
XLA Ops:
  7.8 10.6 %all_gather.24 = bf16[32,2048]{1,0:T(8,128)(2,1)S(1)} all-gather(bf16[32,512]{1,0:T(8,128)(2,1)} %param.16), channel_id=1, replica_groups=mesh['tok'=64,'head'=4] {'head'}, dimensions={1}, use_global_device_ids=true | all-gather | bytes 163840 | tf_op jit(solution)/shard_map/all_gather | solution.py:77
  20.8 1.3 fusion.45
  22.1 9.5 %all-gather = f32[128,576]{1,0:T(8,128)S(1)} all-gather(f32[32,576]{1,0:T(8,128)S(1)} %fusion.45), channel_id=2, replica_groups=mesh['tok'=64,'head'=4] {'head'}, dimensions={0}, use_global_device_ids=true | all-gather | bytes 368640 | tf_op jit(solution)/shard_map/all_gather | solution.py:85
  32.8 1.3 fusion.16
  34.0 1.4 multiply_cosine_fusion
  35.5 1.0 subtract_convert_fusion
  37.3 1.3 dynamic-slice
  39.2 0.9 dynamic-update-slice
  41.0 251.0 %all-reduce.6 = (s32[2048]{0:T(1024)S(1)}, s32[2048]{0:T(1024)S(1)}) all-reduce(s32[2048]{0:T(1024)S(1)} %dynamic-update-slice.1, s32[2048]{0:T(1024)S(1)} %dynamic-update-slice), channel_id=1, replica_groups=mesh['tok'=64,'head'=4] {'tok'}, use_global_device_ids=true, to_apply=%add.4 | all-reduce | flops 4096 | bytes 32768
  294.4 2.4 copy.92
  296.8 14.8 %copy.84 = bf16[2048,4,576]{2,1,0:T(4,128)(2,1)} copy(bf16[2048,4,576]{2,0,1:T(8,128)(2,1)} %all-gather.4.cloned.1.call-done) | data formatting | bytes 18874368 | tf_op jit(solution)/shard_map/all_gather | solution.py:118
  311.6 4.7 gather_fusion.1
  316.3 10.5 %all-gather.1 = bf16[32,16,576]{2,0,1:T(8,128)(2,1)S(1)} all-gather(bf16[32,4,576]{2,0,1:T(8,128)(2,1)S(1)} %copy.85), channel_id=3, replica_groups=mesh['tok'=64,'head'=4] {'head'}, dimensions={1}, use_global_device_ids=true | all-gather | bytes 737280 | tf_op jit(solution)/shard_map/all_gather | solution.py:134
  327.0 6.3 %convert_reduce_fusion = (f32[512]{0:T(512)S(1)}, bf16[512,2496]{0,1:T(8,128)(2,1)}) fusion(pred[512,2496]{0,1:T(32,128)(4,1)S(1)} %copy-done.1, bf16[512,576]{1,0:T(8,128)(2,1)S(1)} %bitcast.76, bf16[2496,576]{0,1:T(8,128)(2,1)} %param.23), kind=kOutput, calls=%fused_computation.11 | convolution fusion | flops 1478589952 | bytes 7301120 | tf_op jit(solution)/shard_map/qc,pc->qp/dot_general | solution.py:37
  333.3 4.4 copy.87
  337.7 4.1 fusion
  341.9 1.6 copy.89
  348.3 13.9 %all-reduce.5 = f32[32,16]{1,0:T(8,128)S(1)} all-reduce(f32[32,16]{1,0:T(8,128)S(1)} %reduce_sum.120), channel_id=5, replica_groups=mesh['tok'=64,'head'=4] {'head'}, use_global_device_ids=true, to_apply=%region_11.12.clone | all-reduce | flops 512 | bytes 4096
  362.3 1.2 gather_fusion.5
  363.5 15.3 %all-to-all-start.1 = ((f32[64,1,4]{2,1,0:T(1,128)}), f32[64,1,4]{2,1,0:T(1,128)S(1)}, u32[]{:S(2)}, u32[]{:S(2)}) async-start(f32[64,1,4]{2,1,0:T(1,128)} %bitcast.19), calls=%async_computation.2 | async-start | bytes 65536 | tf_op jit(solution)/shard_map/all_to_all | solution.py:158
  378.9 1.1 copy.90
  380.1 1.6 gather_fusion.3
  381.8 6.4 %all-to-all-done.1 = f32[64,1,4]{2,1,0:T(1,128)S(1)} async-done(((f32[64,1,4]{2,1,0:T(1,128)}), f32[64,1,4]{2,1,0:T(1,128)S(1)}, u32[]{:S(2)}, u32[]{:S(2)}) %all-to-all-start.1) | async-done | bytes 1056 | tf_op jit(solution)/shard_map/all_to_all | solution.py:158
  388.2 5.5 all-to-all-start
  394.7 1.6 gather_fusion.9
  399.3 11.6 %all-to-all-done = f32[64,1,4,512]{3,2,1,0:T(4,128)} async-done(((f32[64,1,4,512]{3,2,1,0:T(4,128)}), f32[64,1,4,512]{3,2,1,0:T(4,128)}, u32[]{:S(2)}, u32[]{:S(2)}) %all-to-all-start) | async-done | bytes 524320 | tf_op jit(solution)/shard_map/all_to_all | solution.py:151
  410.9 1.9 gather_fusion.4
  412.8 1.1 fusion.29
  413.9 1.2 fusion.17
  415.2 2.8 fusion.40
  419.0 15.0 %reduce-scatter.7.cloned.1.call-done = f32[32,512]{1,0:T(8,128)} async-done(((f32[32,2048]{1,0:T(8,128)}), f32[32,512]{1,0:T(8,128)}) %reduce-scatter.7.cloned.1.call-update) | async-done | bytes 65552 | tf_op jit(solution)/shard_map/reduce_scatter | solution.py:177
  434.0 1.0 fusion.37
  435.8 11.8 %all-reduce.7 = (f32[32]{0:T(128)S(1)}, f32[32,64]{1,0:T(8,128)S(1)}) all-reduce(f32[32]{0:T(128)S(1)} %get-tuple-element.13, f32[32,64]{1,0:T(8,128)S(1)} %fusion.38), channel_id=1, replica_groups=mesh['tok'=64,'head'=4] {'head'}, use_global_device_ids=true, to_apply=%region_15.16 | all-reduce | flops 2080 | bytes 16640 | tf_op jit(solution)/shard_map/psum | solution.py:186
  447.7 9.3 %all_gather.31 = bf16[32,2048]{1,0:T(8,128)(2,1)S(1)} all-gather(bf16[32,512]{1,0:T(8,128)(2,1)S(1)} %fusion.36), channel_id=1, replica_groups=mesh['tok'=64,'head'=4] {'head'}, dimensions={1}, use_global_device_ids=true | all-gather | bytes 163840 | tf_op jit(solution)/shard_map/all_gather | solution.py:213
  457.0 3.1 gather_fusion.7
  460.1 3.7 reshape.358
  463.9 70.4 %all_to_all.20 = bf16[64,6,2048]{2,1,0:T(8,128)(2,1)} all-to-all(bf16[64,6,2048]{2,1,0:T(8,128)(2,1)} %reshape.358), channel_id=1, replica_groups=mesh['tok'=64,'head'=4] {'tok'}, dimensions={0} | all-to-all | bytes 3145728 | tf_op jit(solution)/shard_map/all_to_all | solution.py:217
  534.3 3.7 reshape.359
  538.0 3.6 fusion.8
  541.6 5.5 convolution_convert_fusion
  547.9 21.6 %reduce-scatter.9.cloned.1.call-done = bf16[384,512]{1,0:T(8,128)(2,1)} async-done(((bf16[384,2048]{1,0:T(8,128)(2,1)}), bf16[384,512]{1,0:T(8,128)(2,1)}) %reduce-scatter.9.cloned.1.call-update) | async-done | bytes 393232 | tf_op jit(solution)/shard_map/reduce_scatter | solution.py:228
  569.5 1.9 reshape.360
  571.4 11.7 %all-to-all-start.3 = ((bf16[64,6,512]{2,1,0:T(8,128)(2,1)}), bf16[64,6,512]{2,1,0:T(8,128)(2,1)}, u32[]{:S(2)}, u32[]{:S(2)}) async-start(bf16[64,6,512]{2,1,0:T(8,128)(2,1)} %reshape.360), calls=%async_computation.6 | async-start | bytes 1048576 | tf_op jit(solution)/shard_map/all_to_all | solution.py:234
  584.2 16.2 %all-to-all-done.3 = bf16[64,6,512]{2,1,0:T(8,128)(2,1)} async-done(((bf16[64,6,512]{2,1,0:T(8,128)(2,1)}), bf16[64,6,512]{2,1,0:T(8,128)(2,1)}, u32[]{:S(2)}, u32[]{:S(2)}) %all-to-all-start.3) | async-done | bytes 393248 | tf_op jit(solution)/shard_map/all_to_all | solution.py:234
  600.4 1.2 reshape.361
  601.5 1.7 gather_fusion.8
  603.2 1.8 reshape.446
  605.0 1.9 multiply_reduce_fusion
  (146 shorter events, 20.4 us)
Async XLA Ops:
  7.2 12.2 %copy-start = (bf16[2048,768]{1,0:T(8,128)(2,1)S(1)}, bf16[2048,768]{1,0:T(8,128)(2,1)}, u32[]{:S(2)}) copy-start(bf16[2048,768]{1,0:T(8,128)(2,1)} %param.18) | copy-start | bytes 9437188
  7.2 289.6 %all-gather.4.cloned.1.call-start = ((), (), s32[]{:S(2)}) async-start(), calls=%async_computation.7 | async-start | bytes 10649600 | tf_op jit(solution)/shard_map/all_gather | solution.py:118
  19.3 12.3 %copy-start.25 = (s32[32]{0:T(128)S(1)}, s32[32]{0:T(128)}, u32[]{:S(2)}) copy-start(s32[32]{0:T(128)} %param.24) | copy-start | bytes 388
  37.3 341.7 %reduce-scatter.5.cloned.1.call-start = ((), (), s32[]{:S(2)}) async-start(), calls=%async_computation.8 | async-start | bytes 1310720 | tf_op jit(solution)/shard_map/reduce_scatter | solution.py:139
  292.0 4.8 copy-start.11
  292.2 0.7 copy-start.22
  292.2 19.3 %copy-start.19 = (s32[1024]{0:T(1024)}, s32[1024]{0:T(1024)S(1)}, u32[]{:S(2)}) copy-start(s32[1024]{0:T(1024)S(1)} %pad_clamp_fusion.4) | copy-start | bytes 12292
  293.4 0.6 copy-start.3
  316.3 10.7 %copy-start.1 = (pred[512,2496]{0,1:T(32,128)(4,1)S(1)}, pred[512,2496]{0,1:T(32,128)(4,1)}, u32[]{:S(2)}) copy-start(pred[512,2496]{0,1:T(32,128)(4,1)} %copy.92) | copy-start | bytes 3833860
  333.3 4.4 copy-start.4
  341.8 1.7 copy-start.12
  341.8 2.9 copy-start.16
  341.8 3.0 copy-start.27
  341.9 4.2 copy-start.23
  341.9 4.3 copy-start.26
  344.8 17.4 %copy-start.8 = (s32[32,6]{1,0:T(8,128)}, s32[32,6]{1,0:T(8,128)S(1)}, u32[]{:S(2)}) copy-start(s32[32,6]{1,0:T(8,128)S(1)} %copy.97) | copy-start | bytes 2308
  363.5 24.7 %all-to-all-start.1 = ((f32[64,1,4]{2,1,0:T(1,128)}), f32[64,1,4]{2,1,0:T(1,128)S(1)}, u32[]{:S(2)}, u32[]{:S(2)}) async-start(f32[64,1,4]{2,1,0:T(1,128)} %bitcast.19), calls=%async_computation.2 | async-start | bytes 65536 | tf_op jit(solution)/shard_map/all_to_all | solution.py:158
  378.9 14.8 %copy-start.24 = (s32[32]{0:T(128)S(1)}, s32[32]{0:T(128)}, u32[]{:S(2)}) copy-start(s32[32]{0:T(128)} %compare_select_fusion.3) | copy-start | bytes 388
  388.2 22.8 %all-to-all-start = ((f32[64,1,4,512]{3,2,1,0:T(4,128)}), f32[64,1,4,512]{3,2,1,0:T(4,128)}, u32[]{:S(2)}, u32[]{:S(2)}) async-start(f32[64,1,4,512]{3,2,1,0:T(4,128)} %bitcast.73), calls=%async_computation.1 | async-start | bytes 1048576 | tf_op jit(solution)/shard_map/all_to_all | solution.py:151
  393.7 40.3 %reduce-scatter.7.cloned.1.call-start = ((), (), s32[]{:S(2)}) async-start(), calls=%async_computation.9 | async-start | bytes 327680 | tf_op jit(solution)/shard_map/reduce_scatter | solution.py:177
  393.7 4.4 copy-start.20
  394.6 2.4 copy-start.21
  394.7 3.1 copy-start.13
  394.7 3.1 copy-start.14
  394.7 3.1 copy-start.2
  397.7 13.2 %copy-start.6 = (bf16[32,512]{1,0:T(8,128)(2,1)}, bf16[32,512]{1,0:T(8,128)(2,1)S(1)}, u32[]{:S(2)}) copy-start(bf16[32,512]{1,0:T(8,128)(2,1)S(1)} %get-tuple-element.16) | copy-start | bytes 98308
  410.9 7.1 %copy-start.9 = (s32[32,6]{1,0:T(8,128)S(1)}, s32[32,6]{1,0:T(8,128)}, u32[]{:S(2)}) copy-start(s32[32,6]{1,0:T(8,128)} %copy-done.8) | copy-start | bytes 2308
  412.8 21.2 %copy-start.10 = (bf16[32,512]{1,0:T(8,128)(2,1)S(1)}, bf16[32,512]{1,0:T(8,128)(2,1)}, u32[]{:S(2)}) copy-start(bf16[32,512]{1,0:T(8,128)(2,1)} %param.16) | copy-start | bytes 98308
  412.8 22.1 %copy-start.15 = (bf16[512,64]{0,1:T(8,128)(2,1)S(1)}, bf16[512,64]{0,1:T(8,128)(2,1)}, u32[]{:S(2)}) copy-start(bf16[512,64]{0,1:T(8,128)(2,1)} %param.27) | copy-start | bytes 196612
  413.9 33.7 %copy-start.18 = (f32[512]{0:T(512)S(1)}, f32[512]{0:T(512)}, u32[]{:S(2)}) copy-start(f32[512]{0:T(512)} %param.26) | copy-start | bytes 6148
  417.9 151.6 %reduce-scatter.9.cloned.1.call-start = ((), (), s32[]{:S(2)}) async-start(), calls=%async_computation.10 | async-start | bytes 1966080 | tf_op jit(solution)/shard_map/reduce_scatter | solution.py:228
  435.0 12.7 %copy-start.5 = (bf16[32,512]{1,0:T(8,128)(2,1)}, bf16[32,512]{1,0:T(8,128)(2,1)S(1)}, u32[]{:S(2)}) copy-start(bf16[32,512]{1,0:T(8,128)(2,1)S(1)} %get-tuple-element.14) | copy-start | bytes 98308
  541.6 5.6 copy-start.7
  547.1 36.2 %copy-start.17 = (s32[32,6]{0,1:T(8,128)S(1)}, s32[32,6]{0,1:T(8,128)}, u32[]{:S(2)}) copy-start(s32[32,6]{0,1:T(8,128)} %param.28) | copy-start | bytes 2308
  571.4 28.9 %all-to-all-start.3 = ((bf16[64,6,512]{2,1,0:T(8,128)(2,1)}), bf16[64,6,512]{2,1,0:T(8,128)(2,1)}, u32[]{:S(2)}, u32[]{:S(2)}) async-start(bf16[64,6,512]{2,1,0:T(8,128)(2,1)} %reshape.360), calls=%async_computation.6 | async-start | bytes 1048576 | tf_op jit(solution)/shard_map/all_to_all | solution.py:234
Sparse Core Ops, SparseCore 0:
  37.4 94.7 all-gather.3
  343.6 25.8 reduce-scatter.4
  418.1 15.8 reduce-scatter.6
  547.2 22.2 reduce-scatter.8
